TPU v7x, 32 devices: a whole 2x2x4 slice. The times are simulated.
32 devices in a mesh: dev: 32 (over z, y, x, core).
Axes of the slice: x: 2, y: 2, z: 4, core: 2. Of those that a mesh axis runs over, the one named last changes fastest.
Arguments:
- tiles: bfloat16 [64, 128, 4096], P('dev'), may hold values from -6 to 6
- footprint: int32 [32, 21, 3], P('dev'), may hold values from 0 to 4032, as said below
- classes: int32 [32], P('dev'), may hold values from 0 to 15
- rotations: int32 [32], P('dev'), may hold values from 0 to 31
- references: bfloat16 [1024, 512], P('dev'), may hold values from -6 to 6
Outputs:
- scores: float32 [32, 512], P('dev')
- class_sums: float32 [1024, 512], P('dev')
Inputs may be any that keep to these rules, and one draw needn't show every extreme that they name: Rows and columns of a footprint lie inside the tile (64 and 4032 at most). Of the footprints of one device's particles at most 2 lie in the tiles held by any one device, and one device holds exactly 2 footprints of every device's particles.
All inputs are finite; a program needn't handle non-finite values.
Results may differ from a plain program's by a relative error of at most 0.0047.
Values may be sent and summed in bfloat16 or wider, within the bound.
No kernel may reach another device: no remote copies, remote signals or barrier semaphores. Data moves between devices by JAX's collectives and lax.ppermute only.
A program may use at most 128 MiB of HBM per device.

v0:
```python
import jax
import jax.numpy as jnp
from jax import lax
from jax.sharding import PartitionSpec as P

TILTS = 21
BOX = 64
CYCLES = 16
ROTS = 32
CLASSES = 16


def back_matrix(count):
    center = (BOX - 1) / 2.0
    tilt = jnp.arange(count, dtype=jnp.float32)[:, None, None, None]
    pixel = jnp.arange(BOX, dtype=jnp.float32)[None, :, None, None]
    xpos = jnp.arange(BOX, dtype=jnp.float32)[None, None, :, None]
    zpos = jnp.arange(BOX, dtype=jnp.float32)[None, None, None, :]
    theta = (-60.0 + 120.0 * tilt / (TILTS - 1)) * (jnp.pi / 180.0)
    place = (xpos - center) * jnp.cos(theta) + (zpos - center) * jnp.sin(theta) + center
    weight = jnp.maximum(0.0, 1.0 - jnp.abs(place - pixel))
    weight = jnp.where(tilt < TILTS, weight, 0.0) / TILTS
    return weight.reshape(count * BOX, BOX * BOX).astype(jnp.bfloat16)


def cyl_matrix():
    center = (BOX - 1) / 2.0
    xpos = jnp.arange(BOX, dtype=jnp.float32)[:, None, None, None]
    zpos = jnp.arange(BOX, dtype=jnp.float32)[None, :, None, None]
    angle = jnp.arange(ROTS, dtype=jnp.float32)[None, None, :, None] * (2.0 * jnp.pi / ROTS)
    radius = (jnp.arange(CYCLES, dtype=jnp.float32)[None, None, None, :] + 0.5) * (
        BOX / (2.0 * CYCLES)
    )
    wx = jnp.maximum(0.0, 1.0 - jnp.abs(xpos - center - radius * jnp.cos(angle)))
    wz = jnp.maximum(0.0, 1.0 - jnp.abs(zpos - center - radius * jnp.sin(angle)))
    return (wx * wz).reshape(BOX * BOX, ROTS * CYCLES).astype(jnp.bfloat16)


def shift_table():
    steps = jnp.arange(ROTS, dtype=jnp.int32)
    want = (steps[None, :, None] - steps[:, None, None]) % ROTS
    return (steps[None, None, :] == want).astype(jnp.float32)


def cut_many(tiles, items):
    flat = items.reshape(-1, 3)

    def cut(item):
        return lax.dynamic_slice(tiles, (item[0], item[1], item[2]), (1, BOX, BOX)).reshape(
            BOX * BOX
        )

    pieces = jax.vmap(cut)(flat)
    return pieces.reshape(items.shape[:-1] + (BOX * BOX,))


def per_device(tiles, footprint, classes, rotations, references):
    ndev = lax.axis_size("dev")
    count = footprint.shape[0]
    asks = count * TILTS
    cap = (2 * asks + ndev - 1) // ndev
    held = tiles.shape[0]
    flat = footprint.reshape(asks, 3)
    owner = flat[:, 0] // held
    local = flat[:, 0] - owner * held
    hits = (owner[:, None] == jnp.arange(ndev, dtype=jnp.int32)[None, :]).astype(jnp.int32)
    slot = jnp.sum((jnp.cumsum(hits, axis=0) - hits) * hits, axis=1)
    wanted = (
        jnp.zeros((ndev, cap, 3), jnp.int32)
        .at[owner, slot]
        .set(jnp.stack([local, flat[:, 1], flat[:, 2]], axis=-1))
    )
    patches_cut = cut_many(
        tiles, lax.all_to_all(wanted, "dev", split_axis=0, concat_axis=0, tiled=True)
    )
    arrived = lax.all_to_all(patches_cut, "dev", split_axis=0, concat_axis=0, tiled=True)
    patch = arrived[owner, slot].reshape(count, TILTS, BOX, BOX)
    padded = TILTS + TILTS % 2
    pmat = patch.transpose(0, 2, 1, 3)
    pmat = jnp.pad(pmat, ((0, 0), (0, 0), (0, padded - TILTS), (0, 0))).reshape(
        count * BOX, padded * BOX
    )
    volume = jnp.dot(pmat, back_matrix(padded), preferred_element_type=jnp.float32).astype(
        jnp.bfloat16
    )
    cyl = jnp.dot(volume, cyl_matrix(), preferred_element_type=jnp.float32).astype(jnp.bfloat16)
    cyl = cyl.reshape(count, BOX, ROTS * CYCLES)
    whole_refs = lax.all_gather(references, "dev", axis=0, tiled=True)
    ref_three = (
        whole_refs.reshape(CLASSES, BOX, ROTS, CYCLES)
        .transpose(0, 2, 1, 3)
        .reshape(CLASSES, ROTS, BOX * CYCLES)
    )
    ref_float = whole_refs.astype(jnp.float32).reshape(CLASSES, BOX * ROTS * CYCLES)
    ref_power = jnp.mean(ref_float * ref_float, axis=1)
    cyl_three = (
        cyl.reshape(count, BOX, ROTS, CYCLES)
        .transpose(0, 2, 1, 3)
        .reshape(count, ROTS, BOX * CYCLES)
    )
    corr = jnp.einsum("pfm,cgm->pcfg", cyl_three, ref_three, preferred_element_type=jnp.float32)
    raw = jnp.einsum("pcfg,kfg->pck", corr, shift_table(), precision=lax.Precision.HIGHEST)
    cyl_float = cyl.astype(jnp.float32)
    power = jnp.mean(cyl_float.reshape(count, -1) ** 2, axis=1)
    total = BOX * ROTS * CYCLES
    scores = raw / jnp.sqrt(
        total * (power[:, None, None] + 1e-06) * (ref_power[None, :, None] + 1e-06)
    )
    scores = scores.reshape(count, CLASSES * ROTS)
    columns = jnp.arange(ROTS * CYCLES, dtype=jnp.int32)
    index = (columns[None, :] + rotations[:, None] * CYCLES) % (ROTS * CYCLES)
    turned = jnp.take_along_axis(cyl, index[:, None, :], axis=2)
    member = (classes[:, None] == jnp.arange(CLASSES, dtype=jnp.int32)[None, :]).astype(
        jnp.bfloat16
    )
    owned = CLASSES * BOX // ndev
    placed = member[:, :, None, None] * turned[:, None, :, :]
    placed = placed.reshape(count, ndev, owned, ROTS * CYCLES)
    landed = lax.all_to_all(placed, "dev", split_axis=1, concat_axis=0, tiled=True)
    class_sums = jnp.sum(landed.astype(jnp.float32), axis=(0, 1))
    return (scores, class_sums)


def solution(mesh):
    in_specs = (P("dev", None, None), P("dev", None, None), P("dev"), P("dev"), P("dev", None))
    out_specs = (P("dev", None), P("dev", None))
    return jax.shard_map(
        per_device, mesh=mesh, in_specs=in_specs, out_specs=out_specs, check_vma=False
    )
```

profile of v0, /device:TPU:0, one launch (start us, length us, event | category | flops | bytes accessed | tf_op | source)
XLA Modules:
  0.0 373.9 jit_solution(16164082664645555117)
XLA Ops:
  8.9 4.0 %scatter_fusion = s32[32,2,3]{2,1,0:T(2,128)} fusion(s32[32,2,3]{2,1,0:T(2,128)} %broadcast_in_dim.14, s32[21]{0:T(128)S(1)} %get-tuple-element.20, s32[21,3]{1,0:T(8,128)S(1)} %copy.36), kind=kCustom, calls=%fused_computation.2 | custom fusion | bytes 924 | tf_op jit(solution)/shard_map/scatter | solution.py:71
  12.9 7.3 %all-to-all-start = ((s32[32,2,3]{2,1,0:T(2,128)}), s32[32,2,3]{2,1,0:T(2,128)S(1)}, u32[]{:S(2)}, u32[]{:S(2)}) async-start(s32[32,2,3]{2,1,0:T(2,128)} %scatter_fusion), calls=%async_computation | async-start | bytes 65536 | tf_op jit(solution)/shard_map/all_to_all | solution.py:74
  21.4 13.3 %multiply_convert_fusion = bf16[22,64,64,64]{3,2,1,0:T(8,128)(2,1)} fusion(f32[22,64,64]{2,1,0:T(8,128)S(1)} %add_add_fusion, pred[22]{0:T(512)(128)(4,1)S(1)} %iota_compare_fusion.3), kind=kLoop, calls=%fused_computation.5 | loop fusion | flops 40370176 | bytes 11894806 | tf_op jit(solution)/shard_map/convert_element_type | solution.py:23
  35.4 224.2 %while.1 = (s32[]{:T(128)}, bf16[2,128,4096]{2,1,0:T(8,128)(2,1)}, s32[64,3]{0,1:T(4,128)S(1)}, bf16[64,1,64,64]{3,2,1,0:T(8,128)(2,1)S(1)}, s32[]{:T(128)}) while((s32[]{:T(128)}, bf16[2,128,4096]{2,1,0:T(8,128)(2,1)}, s32[64,3]{0,1:T(4,128)S(1)}, bf16[64,1,64,64]{3,2,1,0:T(8,128)(2,1)S(1)}, s32[]{:T(128)}) %tuple.35), condition=%wide.while_cond, body=%wide.while_body.sunk | while | flops 2 | bytes 24705 | solution.py:49
  36.0 2.8 bitcast_dynamic-update-slice_fusion.2
  39.5 2.8 bitcast_dynamic-update-slice_fusion.2
  57.1 2.8 bitcast_dynamic-update-slice_fusion.2
  60.6 2.8 bitcast_dynamic-update-slice_fusion.2
  64.1 2.8 bitcast_dynamic-update-slice_fusion.2
  67.6 2.8 bitcast_dynamic-update-slice_fusion.2
  71.1 2.8 bitcast_dynamic-update-slice_fusion.2
  78.1 2.8 bitcast_dynamic-update-slice_fusion.2
  81.6 2.8 bitcast_dynamic-update-slice_fusion.2
  85.1 2.8 bitcast_dynamic-update-slice_fusion.2
  88.6 2.8 bitcast_dynamic-update-slice_fusion.2
  92.1 2.8 bitcast_dynamic-update-slice_fusion.2
  109.6 2.8 bitcast_dynamic-update-slice_fusion.2
  113.1 2.8 bitcast_dynamic-update-slice_fusion.2
  116.6 2.8 bitcast_dynamic-update-slice_fusion.2
  120.1 2.8 bitcast_dynamic-update-slice_fusion.2
  123.6 2.8 bitcast_dynamic-update-slice_fusion.2
  144.6 2.8 bitcast_dynamic-update-slice_fusion.2
  148.2 2.8 bitcast_dynamic-update-slice_fusion.2
  261.1 5.8 %all-to-all-start.1 = ((bf16[32,2,4096]{2,1,0:T(2,128)(2,1)}), bf16[32,2,4096]{2,1,0:T(2,128)(2,1)S(1)}, u32[]{:S(2)}, u32[]{:S(2)}) async-start(bf16[32,2,4096]{2,1,0:T(2,128)(2,1)} %reshape.573), calls=%async_computation.1 | async-start | bytes 1048576 | tf_op jit(solution)/shard_map/all_to_all | solution.py:76
  266.9 7.3 %multiply_convert_fusion.1 = bf16[64,64,32,16]{1,0,3,2:T(8,128)(2,1)} fusion(f32[64,32,16]{0,2,1:T(8,128)S(1)} %get-tuple-element.31, f32[64,32,16]{0,2,1:T(8,128)S(1)} %get-tuple-element.30), kind=kLoop, calls=%fused_computation.6 | loop fusion | flops 4194304 | bytes 4456448 | tf_op jit(solution)/shard_map/convert_element_type | solution.py:36
  274.3 12.1 %convert_element_type.63 = bf16[4096,512]{0,1:T(8,128)(2,1)} reshape(bf16[64,64,32,16]{1,0,3,2:T(8,128)(2,1)} %multiply_convert_fusion.1) | data formatting | bytes 8388608 | tf_op jit(solution)/shard_map/convert_element_type | solution.py:36
  286.3 30.6 %convert_element_type.60 = bf16[1408,4096]{1,0:T(8,128)(2,1)} reshape(bf16[22,64,64,64]{3,2,1,0:T(8,128)(2,1)} %multiply_convert_fusion) | data formatting | bytes 23068672 | tf_op jit(solution)/shard_map/convert_element_type | solution.py:23
  320.4 9.5 %multiply_reduce_fusion.1 = (f32[]{:T(128)}, bf16[64,512]{1,0:T(8,128)(2,1)S(1)}) fusion(bf16[4096,512]{0,1:T(8,128)(2,1)} %convert_element_type.63, bf16[64,1408]{1,0:T(8,128)(2,1)S(1)} %reshape.575, bf16[1408,4096]{1,0:T(8,128)(2,1)} %convert_element_type.60), kind=kOutput, calls=%fused_computation.23 | convolution fusion | flops 1007026176 | bytes 15974404 | tf_op jit(solution)/shard_map/dot_general | solution.py:86
  332.9 6.1 %all-to-all-start.2 = ((bf16[1,32,32,512]{3,2,0,1:T(8,128)(2,1)}), bf16[1,32,32,512]{3,2,0,1:T(8,128)(2,1)}, u32[]{:S(2)}, u32[]{:S(2)}) async-start(bf16[1,32,32,512]{3,2,0,1:T(8,128)(2,1)} %broadcast_multiply_fusion), calls=%async_computation.2 | async-start | bytes 2097152 | tf_op jit(solution)/shard_map/all_to_all | solution.py:119
  342.9 4.9 %copy.42 = bf16[16,32,64,16]{1,3,2,0:T(8,128)(2,1)} copy(bf16[16,32,64,16]{2,0,3,1:T(8,128)(2,1)S(1)} %bitcast.74) | data formatting | bytes 2097152 | tf_op jit(solution)/shard_map/transpose | solution.py:91
  349.5 3.0 convolution_bitcast_fusion
  353.7 11.4 %all-to-all-done.2 = bf16[1,32,32,512]{3,2,0,1:T(8,128)(2,1)} async-done(((bf16[1,32,32,512]{3,2,0,1:T(8,128)(2,1)}), bf16[1,32,32,512]{3,2,0,1:T(8,128)(2,1)}, u32[]{:S(2)}, u32[]{:S(2)}) %all-to-all-start.2) | async-done | bytes 1048608 | tf_op jit(solution)/shard_map/all_to_all | solution.py:119
  (234 shorter events, 187.7 us)
Async XLA Ops:
  12.9 22.1 %all-to-all-start = ((s32[32,2,3]{2,1,0:T(2,128)}), s32[32,2,3]{2,1,0:T(2,128)S(1)}, u32[]{:S(2)}, u32[]{:S(2)}) async-start(s32[32,2,3]{2,1,0:T(2,128)} %scatter_fusion), calls=%async_computation | async-start | bytes 65536 | tf_op jit(solution)/shard_map/all_to_all | solution.py:74
  20.2 319.8 %all-gather.2.cloned.1.call-start = ((), (), s32[]{:S(2)}) async-start(), calls=%async_computation.3 | async-start | bytes 1081344 | tf_op jit(solution)/shard_map/all_gather | solution.py:88
  261.1 57.3 %all-to-all-start.1 = ((bf16[32,2,4096]{2,1,0:T(2,128)(2,1)}), bf16[32,2,4096]{2,1,0:T(2,128)(2,1)S(1)}, u32[]{:S(2)}, u32[]{:S(2)}) async-start(bf16[32,2,4096]{2,1,0:T(2,128)(2,1)} %reshape.573), calls=%async_computation.1 | async-start | bytes 1048576 | tf_op jit(solution)/shard_map/all_to_all | solution.py:76
  332.9 32.2 %all-to-all-start.2 = ((bf16[1,32,32,512]{3,2,0,1:T(8,128)(2,1)}), bf16[1,32,32,512]{3,2,0,1:T(8,128)(2,1)}, u32[]{:S(2)}, u32[]{:S(2)}) async-start(bf16[1,32,32,512]{3,2,0,1:T(8,128)(2,1)} %broadcast_multiply_fusion), calls=%async_computation.2 | async-start | bytes 2097152 | tf_op jit(solution)/shard_map/all_to_all | solution.py:119
Sparse Core Ops, SparseCore 0:
  23.9 55.0 all-gather.1
where the time goes:
time: 381 us; the launch traced here: 374 us
  local copies, waits for them, and re-layouts  286 us (75%)
  other arithmetic  26.7 us (7%)
  starting transfers between devices  19.3 us (5%)
  between operations  16.2 us (4%)
  matrix products  13.1 us (3%)
  waiting for transfers between devices  12.1 us (3%)
    gather x192, local copies, waits for them, and re-layouts  223 us
    convert_element_type x1, local copies, waits for them, and re-layouts, back_matrix(): return weight.reshape(count * BOX, BOX * BOX).astype(jnp.bfloat16)  30.6 us
    convert_element_type x1, other arithmetic, back_matrix(): return weight.reshape(count * BOX, BOX * BOX).astype(jnp.bfloat16)  13.3 us
    convert_element_type x1, local copies, waits for them, and re-layouts, cyl_matrix(): return (wx * wz).reshape(BOX * BOX, ROTS * CYCLES).astype(jnp.bfloat16)  12.1 us
    all_to_all x1, waiting for transfers between devices, per_device(): lax.all_to_all(placed, 'dev', split_axis=1, concat_axis=0, tiled=True)  11.4 us
    dot_general x1, matrix products, per_device(): jnp.dot(volume, cyl_matrix(), preferred_element_type=jnp.float32)  9.51 us
  transfers between devices with their start and end apart: 4, of which 1 were waited for; matrix products, arithmetic and copies ran while one was open for 85% of the time, Pallas kernels for 0%

commit v1 on v0

--- a/solution.py
+++ b/solution.py
@@ -116,7 +116,9 @@
     owned = CLASSES * BOX // ndev
     placed = member[:, :, None, None] * turned[:, None, :, :]
     placed = placed.reshape(count, ndev, owned, ROTS * CYCLES)
-    landed = lax.all_to_all(placed, "dev", split_axis=1, concat_axis=0, tiled=True)
+    parts = jnp.split(placed, lax.axis_size("dev"), axis=1)
+    incoming = lax.all_to_all(jnp.stack(parts), "dev", 0, 0)
+    landed = jnp.concatenate(incoming, axis=0)
     class_sums = jnp.sum(landed.astype(jnp.float32), axis=(0, 1))
     return (scores, class_sums)
 

time: 381 us -> 400 us (1.050)
  local copies, waits for them, and re-layouts: 286 us -> 305 us
    unnamed x4 -> x35, local copies, waits for them, and re-layouts: 0.9 us -> 19.6 us
  transfers between devices with their start and end apart: 4 -> 4, of which waited for: 1 -> 1; matrix products, arithmetic and copies ran while one was open for 85% -> 86% of each run, Pallas kernels for 0% -> 0%
where the time goes in v1:
time: 400 us; the launch traced here: 392 us
  local copies, waits for them, and re-layouts  305 us (76%)
  other arithmetic  25.7 us (6%)
  starting transfers between devices  19.1 us (5%)
  between operations  16.3 us (4%)
  matrix products  13.1 us (3%)
  waiting for transfers between devices  12.2 us (3%)
    gather x192, local copies, waits for them, and re-layouts  223 us
    convert_element_type x1, local copies, waits for them, and re-layouts, back_matrix(): return weight.reshape(count * BOX, BOX * BOX).astype(jnp.bfloat16)  30.6 us
    unnamed x35, local copies, waits for them, and re-layouts  19.6 us
    convert_element_type x1, other arithmetic, back_matrix(): return weight.reshape(count * BOX, BOX * BOX).astype(jnp.bfloat16)  13.3 us
    convert_element_type x1, local copies, waits for them, and re-layouts, cyl_matrix(): return (wx * wz).reshape(BOX * BOX, ROTS * CYCLES).astype(jnp.bfloat16)  12.1 us
    all_to_all x1, waiting for transfers between devices, per_device(): incoming = lax.all_to_all(jnp.stack(parts), 'dev', 0, 0)  11.5 us
    dot_general x1, matrix products, per_device(): jnp.dot(volume, cyl_matrix(), preferred_element_type=jnp.float32)  9.51 us
  transfers between devices with their start and end apart: 4, of which 1 were waited for; matrix products, arithmetic and copies ran while one was open for 86% of the time, Pallas kernels for 0%

profile of v1, /device:TPU:0, one launch (start us, length us, event | category | flops | bytes accessed | tf_op | source)
XLA Modules:
  0.0 392.3 jit_solution(16512875470035786563)
XLA Ops:
  8.9 4.0 %scatter_fusion = s32[32,2,3]{2,1,0:T(2,128)} fusion(s32[32,2,3]{2,1,0:T(2,128)} %broadcast_in_dim.14, s32[21]{0:T(128)S(1)} %get-tuple-element.20, s32[21,3]{1,0:T(8,128)S(1)} %copy.24), kind=kCustom, calls=%fused_computation.2 | custom fusion | bytes 924 | tf_op jit(solution)/shard_map/scatter | solution.py:71
  12.9 7.3 %all-to-all-start = ((s32[32,2,3]{2,1,0:T(2,128)}), s32[32,2,3]{2,1,0:T(2,128)S(1)}, u32[]{:S(2)}, u32[]{:S(2)}) async-start(s32[32,2,3]{2,1,0:T(2,128)} %scatter_fusion), calls=%async_computation | async-start | bytes 65536 | tf_op jit(solution)/shard_map/all_to_all | solution.py:74
  21.4 13.3 %multiply_convert_fusion = bf16[22,64,64,64]{3,2,1,0:T(8,128)(2,1)} fusion(f32[22,64,64]{2,1,0:T(8,128)S(1)} %add_add_fusion, pred[22]{0:T(512)(128)(4,1)S(1)} %iota_compare_fusion.3), kind=kLoop, calls=%fused_computation.5 | loop fusion | flops 40370176 | bytes 11894806 | tf_op jit(solution)/shard_map/convert_element_type | solution.py:23
  35.4 224.2 %while.1 = (s32[]{:T(128)}, bf16[2,128,4096]{2,1,0:T(8,128)(2,1)}, s32[64,3]{0,1:T(4,128)S(1)}, bf16[64,1,64,64]{3,2,1,0:T(8,128)(2,1)S(1)}, s32[]{:T(128)}) while((s32[]{:T(128)}, bf16[2,128,4096]{2,1,0:T(8,128)(2,1)}, s32[64,3]{0,1:T(4,128)S(1)}, bf16[64,1,64,64]{3,2,1,0:T(8,128)(2,1)S(1)}, s32[]{:T(128)}) %tuple.35), condition=%wide.while_cond, body=%wide.while_body.sunk | while | flops 2 | bytes 24705 | solution.py:49
  36.0 2.8 bitcast_dynamic-update-slice_fusion.2
  39.5 2.8 bitcast_dynamic-update-slice_fusion.2
  57.1 2.8 bitcast_dynamic-update-slice_fusion.2
  60.6 2.8 bitcast_dynamic-update-slice_fusion.2
  64.1 2.8 bitcast_dynamic-update-slice_fusion.2
  67.6 2.8 bitcast_dynamic-update-slice_fusion.2
  71.1 2.8 bitcast_dynamic-update-slice_fusion.2
  78.1 2.8 bitcast_dynamic-update-slice_fusion.2
  81.6 2.8 bitcast_dynamic-update-slice_fusion.2
  85.1 2.8 bitcast_dynamic-update-slice_fusion.2
  88.6 2.8 bitcast_dynamic-update-slice_fusion.2
  92.1 2.8 bitcast_dynamic-update-slice_fusion.2
  109.6 2.8 bitcast_dynamic-update-slice_fusion.2
  113.1 2.8 bitcast_dynamic-update-slice_fusion.2
  116.6 2.8 bitcast_dynamic-update-slice_fusion.2
  120.1 2.8 bitcast_dynamic-update-slice_fusion.2
  123.6 2.8 bitcast_dynamic-update-slice_fusion.2
  144.6 2.8 bitcast_dynamic-update-slice_fusion.2
  148.2 2.8 bitcast_dynamic-update-slice_fusion.2
  261.1 5.8 %all-to-all-start.1 = ((bf16[32,2,4096]{2,1,0:T(2,128)(2,1)}), bf16[32,2,4096]{2,1,0:T(2,128)(2,1)S(1)}, u32[]{:S(2)}, u32[]{:S(2)}) async-start(bf16[32,2,4096]{2,1,0:T(2,128)(2,1)} %reshape.571), calls=%async_computation.1 | async-start | bytes 1048576 | tf_op jit(solution)/shard_map/all_to_all | solution.py:76
  266.9 7.3 %multiply_convert_fusion.1 = bf16[64,64,32,16]{1,0,3,2:T(8,128)(2,1)} fusion(f32[64,32,16]{0,2,1:T(8,128)S(1)} %get-tuple-element.31, f32[64,32,16]{0,2,1:T(8,128)S(1)} %get-tuple-element.30), kind=kLoop, calls=%fused_computation.6 | loop fusion | flops 4194304 | bytes 4456448 | tf_op jit(solution)/shard_map/convert_element_type | solution.py:36
  274.3 12.1 %convert_element_type.63 = bf16[4096,512]{0,1:T(8,128)(2,1)} reshape(bf16[64,64,32,16]{1,0,3,2:T(8,128)(2,1)} %multiply_convert_fusion.1) | data formatting | bytes 8388608 | tf_op jit(solution)/shard_map/convert_element_type | solution.py:36
  286.3 30.6 %convert_element_type.60 = bf16[1408,4096]{1,0:T(8,128)(2,1)} reshape(bf16[22,64,64,64]{3,2,1,0:T(8,128)(2,1)} %multiply_convert_fusion) | data formatting | bytes 23068672 | tf_op jit(solution)/shard_map/convert_element_type | solution.py:23
  320.4 9.5 %multiply_reduce_fusion.1 = (f32[]{:T(128)}, bf16[64,512]{1,0:T(8,128)(2,1)S(1)}) fusion(bf16[4096,512]{0,1:T(8,128)(2,1)} %convert_element_type.63, bf16[64,1408]{1,0:T(8,128)(2,1)S(1)} %reshape.573, bf16[1408,4096]{1,0:T(8,128)(2,1)} %convert_element_type.60), kind=kOutput, calls=%fused_computation.23 | convolution fusion | flops 1007026176 | bytes 15974404 | tf_op jit(solution)/shard_map/dot_general | solution.py:86
  351.3 6.0 %all-to-all-start.2 = ((bf16[32,1,1,32,512]{4,3,2,1,0:T(8,128)(2,1)}), bf16[32,1,1,32,512]{4,3,2,1,0:T(8,128)(2,1)}, u32[]{:S(2)}, u32[]{:S(2)}) async-start(bf16[32,1,1,32,512]{4,3,2,1,0:T(8,128)(2,1)} %constant_dynamic-update-slice_fusion), calls=%async_computation.2 | async-start | bytes 2097152 | tf_op jit(solution)/shard_map/all_to_all | solution.py:120
  361.1 4.9 %copy.30 = bf16[16,32,64,16]{1,3,2,0:T(8,128)(2,1)} copy(bf16[16,32,64,16]{2,0,3,1:T(8,128)(2,1)S(1)} %bitcast.202) | data formatting | bytes 2097152 | tf_op jit(solution)/shard_map/transpose | solution.py:91
  367.7 3.0 convolution_bitcast_fusion
  371.9 11.5 %all-to-all-done.2 = bf16[32,1,1,32,512]{4,3,2,1,0:T(8,128)(2,1)} async-done(((bf16[32,1,1,32,512]{4,3,2,1,0:T(8,128)(2,1)}), bf16[32,1,1,32,512]{4,3,2,1,0:T(8,128)(2,1)}, u32[]{:S(2)}, u32[]{:S(2)}) %all-to-all-start.2) | async-done | bytes 1048608 | tf_op jit(solution)/shard_map/all_to_all | solution.py:120
  (266 shorter events, 206.1 us)
Async XLA Ops:
  12.9 22.1 %all-to-all-start = ((s32[32,2,3]{2,1,0:T(2,128)}), s32[32,2,3]{2,1,0:T(2,128)S(1)}, u32[]{:S(2)}, u32[]{:S(2)}) async-start(s32[32,2,3]{2,1,0:T(2,128)} %scatter_fusion), calls=%async_computation | async-start | bytes 65536 | tf_op jit(solution)/shard_map/all_to_all | solution.py:74
  20.2 338.0 %all-gather.2.cloned.1.call-start = ((), (), s32[]{:S(2)}) async-start(), calls=%async_computation.3 | async-start | bytes 1081344 | tf_op jit(solution)/shard_map/all_gather | solution.py:88
  261.1 57.3 %all-to-all-start.1 = ((bf16[32,2,4096]{2,1,0:T(2,128)(2,1)}), bf16[32,2,4096]{2,1,0:T(2,128)(2,1)S(1)}, u32[]{:S(2)}, u32[]{:S(2)}) async-start(bf16[32,2,4096]{2,1,0:T(2,128)(2,1)} %reshape.571), calls=%async_computation.1 | async-start | bytes 1048576 | tf_op jit(solution)/shard_map/all_to_all | solution.py:76
  351.3 32.2 %all-to-all-start.2 = ((bf16[32,1,1,32,512]{4,3,2,1,0:T(8,128)(2,1)}), bf16[32,1,1,32,512]{4,3,2,1,0:T(8,128)(2,1)}, u32[]{:S(2)}, u32[]{:S(2)}) async-start(bf16[32,1,1,32,512]{4,3,2,1,0:T(8,128)(2,1)} %constant_dynamic-update-slice_fusion), calls=%async_computation.2 | async-start | bytes 2097152 | tf_op jit(solution)/shard_map/all_to_all | solution.py:120
Sparse Core Ops, SparseCore 0:
  23.9 55.0 all-gather.1
